TPU v7x, 128 devices: a whole 4x4x4 slice. The times are simulated.
128 devices in a mesh: grid: 32 (over y, x, core), layer: 4 (over z).
Axes of the slice: x: 4, y: 4, z: 4, core: 2. Of those that a mesh axis runs over, the one named last changes fastest.
Arguments:
- h_blocks: bfloat16 [1024, 8, 128, 128], P('grid', 'layer'), may hold values from -0.09375 to 0.09375
- block_cols: int32 [1024, 8], P('grid', 'layer'), may hold values from 0 to 1023, as said below
- t_now: bfloat16 [131072, 1536], P(('grid', 'layer')), may hold values from -6 to 6
- t_prev: bfloat16 [131072, 1536], P(('grid', 'layer')), may hold values from -6 to 6
Outputs:
- next_term: bfloat16 [131072, 1536], P(('grid', 'layer'))
- after_term: bfloat16 [131072, 1536], P(('grid', 'layer'))
Inputs may be any that keep to these rules, and one draw needn't show every extreme that they name: block_cols[i, 0] = i. With g = i // 32, every block column lies among the block rows g * 32 - 2 to g * 32 + 33 counted cyclically modulo 1024, and both ends of that range are named in every block row.
All inputs are finite; a program needn't handle non-finite values.
Results may differ from a plain program's by a relative error of at most 0.019.
Values may be sent and summed in bfloat16 or wider, within the bound.
No kernel may reach another device: no remote copies, remote signals or barrier semaphores. Data moves between devices by JAX's collectives and lax.ppermute only.
A program may use at most 192 MiB of HBM per device.

v0:
```python
import jax
import jax.numpy as jnp
from jax import lax
from jax.sharding import PartitionSpec as P

KB = 8
HB = 2
NCH = 4


def padded(array, width):
    size, length = (lax.axis_size("grid"), array.shape[0])
    up = [(i, (i + 1) % size) for i in range(size)]
    down = [(j, i) for i, j in up]
    before = lax.ppermute(array[length - width :], "grid", up)
    after = lax.ppermute(array[:width], "grid", down)
    return jnp.concatenate([before, array, after], axis=0)


def own_rows(h_own, rel_own, chunk):
    block_size = h_own.shape[2]
    panel = lax.all_gather(chunk, "layer", axis=0, tiled=True)
    wide = padded(panel, HB * block_size)
    blocks = wide.reshape(wide.shape[0] // block_size, block_size, chunk.shape[1])
    picked = blocks[rel_own]
    acc = jnp.einsum("rsij,rsjc->ric", h_own, picked, preferred_element_type=jnp.float32)
    return acc.reshape(chunk.shape[0], chunk.shape[1])


def shards(h_blocks, block_cols, t_now, t_prev):
    group_rows = h_blocks.shape[0]
    total_blocks = group_rows * lax.axis_size("grid")
    first_block = lax.axis_index("grid") * group_rows
    relative = (block_cols - first_block + HB + total_blocks) % total_blocks
    h_own = lax.all_to_all(h_blocks, "layer", 0, 1, tiled=True)
    rel_own = lax.all_to_all(relative, "layer", 0, 1, tiled=True)
    width = t_now.shape[1]
    step = width // NCH

    def recur(current, previous):
        outs = []
        for c in range(NCH):
            acc = own_rows(h_own, rel_own, current[c])
            outs.append((2.0 * acc - previous[c].astype(jnp.float32)).astype(jnp.bfloat16))
        return outs

    now_chunks = [t_now[:, c * step : (c + 1) * step] for c in range(NCH)]
    prev_chunks = [t_prev[:, c * step : (c + 1) * step] for c in range(NCH)]
    next_chunks = recur(now_chunks, prev_chunks)
    after_chunks = recur(next_chunks, now_chunks)
    return (jnp.concatenate(next_chunks, axis=1), jnp.concatenate(after_chunks, axis=1))


def solution(mesh):
    in_specs = (
        P("grid", "layer", None, None),
        P("grid", "layer"),
        P(("grid", "layer"), None),
        P(("grid", "layer"), None),
    )
    out_specs = (P(("grid", "layer"), None), P(("grid", "layer"), None))
    return jax.shard_map(shards, mesh=mesh, in_specs=in_specs, out_specs=out_specs, check_vma=False)
```

profile of v0, /device:TPU:0, one launch (start us, length us, event | category | flops | bytes accessed | tf_op | source)
XLA Modules:
  0.0 535.9 jit_solution(12677658248927611347)
XLA Ops:
  13.1 10.5 %all_to_all.37 = s32[4,8,2]{1,2,0:T(2,128)S(1)} all-to-all(s32[4,8,2]{1,2,0:T(2,128)S(1)} %copy.9), channel_id=1, replica_groups=mesh['grid'=32,'layer'=4] {'layer'}, dimensions={0} | all-to-all | bytes 512 | tf_op jit(solution)/shard_map/all_to_all | solution.py:36
  27.4 48.1 %all-to-all-done.1 = bf16[32,2,128,128]{3,2,1,0:T(8,128)(2,1)S(1)} async-done(((bf16[32,2,128,128]{3,2,1,0:T(8,128)(2,1)}), bf16[32,2,128,128]{3,2,1,0:T(8,128)(2,1)S(1)}, u32[]{:S(2)}, u32[]{:S(2)}) %all-to-all-start.1) | async-done | bytes 2097184 | tf_op jit(solution)/shard_map/all_to_all | solution.py:35
  84.8 32.1 %all-gather.13.cloned.1.call-done = bf16[4096,384]{1,0:T(8,128)(2,1)} async-done(((bf16[1024,384]{1,0:T(8,128)(2,1)}), bf16[4096,384]{1,0:T(8,128)(2,1)}) %all-gather.13.cloned.1.call-update) | async-done | bytes 3145744 | tf_op jit(solution)/shard_map/all_gather | solution.py:22
  123.8 34.6 %all-gather.11.cloned.1.call-done = bf16[4096,384]{1,0:T(8,128)(2,1)} async-done(((bf16[1024,384]{1,0:T(8,128)(2,1)}), bf16[4096,384]{1,0:T(8,128)(2,1)}) %all-gather.11.cloned.1.call-update) | async-done | bytes 3145744 | tf_op jit(solution)/shard_map/all_gather | solution.py:22
  160.2 40.0 %all-gather.9.cloned.1.call-done = bf16[4096,384]{1,0:T(8,128)(2,1)} async-done(((bf16[1024,384]{1,0:T(8,128)(2,1)}), bf16[4096,384]{1,0:T(8,128)(2,1)}) %all-gather.9.cloned.1.call-update) | async-done | bytes 3145744 | tf_op jit(solution)/shard_map/all_gather | solution.py:22
  206.2 7.1 %pad_maximum_fusion.3 = bf16[4608,384]{1,0:T(8,128)(2,1)} fusion(bf16[256,384]{1,0:T(8,128)(2,1)S(1)} %collective-permute-done.7, bf16[4096,384]{1,0:T(8,128)(2,1)} %all-gather.15.cloned.1.call-done, bf16[256,384]{1,0:T(8,128)(2,1)S(1)} %collective-permute-done.6), kind=kLoop, calls=%fused_computation.11 | loop fusion | flops 10616832 | bytes 7077888 | tf_op jit(solution)/shard_map/concatenate | solution.py:17
  213.3 6.1 %gather_fusion.3 = bf16[64,128,384]{2,1,0:T(8,128)(2,1)} fusion(bf16[36,128,384]{2,1,0:T(8,128)(2,1)} %bitcast.132, s32[1024]{0:T(1024)S(1)} %pad_clamp_fusion), kind=kCustom, calls=%fused_computation.3 | custom fusion | bytes 12583168 | tf_op jit(solution)/shard_map/gather | solution.py:25
  224.9 7.0 %pad_maximum_fusion.2 = bf16[4608,384]{1,0:T(8,128)(2,1)} fusion(bf16[256,384]{1,0:T(8,128)(2,1)S(1)} %collective-permute-done.5, bf16[4096,384]{1,0:T(8,128)(2,1)} %all-gather.13.cloned.1.call-done, bf16[256,384]{1,0:T(8,128)(2,1)S(1)} %collective-permute-done.4), kind=kLoop, calls=%fused_computation.10 | loop fusion | flops 10616832 | bytes 7077888 | tf_op jit(solution)/shard_map/concatenate | solution.py:17
  232.0 6.1 %gather_fusion.2 = bf16[64,128,384]{2,1,0:T(8,128)(2,1)} fusion(bf16[36,128,384]{2,1,0:T(8,128)(2,1)} %bitcast.133, s32[1024]{0:T(1024)S(1)} %pad_clamp_fusion), kind=kCustom, calls=%fused_computation.2 | custom fusion | bytes 12583168 | tf_op jit(solution)/shard_map/gather | solution.py:25
  245.9 6.3 %pad_maximum_fusion.1 = bf16[4608,384]{1,0:T(8,128)(2,1)} fusion(bf16[256,384]{1,0:T(8,128)(2,1)S(1)} %collective-permute-done.3, bf16[4096,384]{1,0:T(8,128)(2,1)S(1)} %copy-done.11, bf16[256,384]{1,0:T(8,128)(2,1)S(1)} %collective-permute-done.2), kind=kLoop, calls=%fused_computation.9 | loop fusion | flops 10616832 | bytes 7077888 | tf_op jit(solution)/shard_map/concatenate | solution.py:17
  252.2 6.1 %gather_fusion.1 = bf16[64,128,384]{2,1,0:T(8,128)(2,1)} fusion(bf16[36,128,384]{2,1,0:T(8,128)(2,1)} %bitcast.134, s32[1024]{0:T(1024)S(1)} %pad_clamp_fusion), kind=kCustom, calls=%fused_computation.1 | custom fusion | bytes 12583168 | tf_op jit(solution)/shard_map/gather | solution.py:25
  263.6 6.5 %pad_maximum_fusion = bf16[4608,384]{1,0:T(8,128)(2,1)} fusion(bf16[256,384]{1,0:T(8,128)(2,1)S(1)} %collective-permute-done.1, bf16[4096,384]{1,0:T(8,128)(2,1)S(1)} %copy-done.10, bf16[256,384]{1,0:T(8,128)(2,1)S(1)} %collective-permute-done), kind=kLoop, calls=%fused_computation.8 | loop fusion | flops 10616832 | bytes 7077888 | tf_op jit(solution)/shard_map/concatenate | solution.py:17
  270.1 6.1 %gather_fusion = bf16[64,128,384]{2,1,0:T(8,128)(2,1)} fusion(bf16[36,128,384]{2,1,0:T(8,128)(2,1)} %bitcast.135, s32[1024]{0:T(1024)S(1)} %pad_clamp_fusion), kind=kCustom, calls=%fused_computation | custom fusion | bytes 12583168 | tf_op jit(solution)/shard_map/gather | solution.py:25
  288.6 29.9 %all-gather.23.cloned.1.call-done = bf16[4096,384]{1,0:T(8,128)(2,1)} async-done(((bf16[1024,384]{1,0:T(8,128)(2,1)}), bf16[4096,384]{1,0:T(8,128)(2,1)}) %all-gather.23.cloned.1.call-update) | async-done | bytes 3145744 | tf_op jit(solution)/shard_map/all_gather | solution.py:22
  324.7 35.1 %all-gather.21.cloned.1.call-done = bf16[4096,384]{1,0:T(8,128)(2,1)} async-done(((bf16[1024,384]{1,0:T(8,128)(2,1)}), bf16[4096,384]{1,0:T(8,128)(2,1)}) %all-gather.21.cloned.1.call-update) | async-done | bytes 3145744 | tf_op jit(solution)/shard_map/all_gather | solution.py:22
  366.7 34.6 %all-gather.19.cloned.1.call-done = bf16[4096,384]{1,0:T(8,128)(2,1)} async-done(((bf16[1024,384]{1,0:T(8,128)(2,1)}), bf16[4096,384]{1,0:T(8,128)(2,1)}) %all-gather.19.cloned.1.call-update) | async-done | bytes 3145744 | tf_op jit(solution)/shard_map/all_gather | solution.py:22
  403.1 40.2 %all-gather.17.cloned.1.call-done = bf16[4096,384]{1,0:T(8,128)(2,1)} async-done(((bf16[1024,384]{1,0:T(8,128)(2,1)}), bf16[4096,384]{1,0:T(8,128)(2,1)}) %all-gather.17.cloned.1.call-update) | async-done | bytes 3145744 | tf_op jit(solution)/shard_map/all_gather | solution.py:22
  449.2 7.1 %pad_maximum_fusion.7 = bf16[4608,384]{1,0:T(8,128)(2,1)} fusion(bf16[256,384]{1,0:T(8,128)(2,1)S(1)} %collective-permute-done.15, bf16[4096,384]{1,0:T(8,128)(2,1)} %all-gather.23.cloned.1.call-done, bf16[256,384]{1,0:T(8,128)(2,1)S(1)} %collective-permute-done.14), kind=kLoop, calls=%fused_computation.15 | loop fusion | flops 10616832 | bytes 7077888 | tf_op jit(solution)/shard_map/concatenate | solution.py:17
  456.3 6.1 %gather_fusion.7 = bf16[64,128,384]{2,1,0:T(8,128)(2,1)} fusion(bf16[36,128,384]{2,1,0:T(8,128)(2,1)} %bitcast.136, s32[1024]{0:T(1024)S(1)} %pad_clamp_fusion), kind=kCustom, calls=%fused_computation.7 | custom fusion | bytes 12583168 | tf_op jit(solution)/shard_map/gather | solution.py:25
  472.8 6.5 %pad_maximum_fusion.6 = bf16[4608,384]{1,0:T(8,128)(2,1)} fusion(bf16[256,384]{1,0:T(8,128)(2,1)S(1)} %collective-permute-done.13, bf16[4096,384]{1,0:T(8,128)(2,1)S(1)} %copy-done.14, bf16[256,384]{1,0:T(8,128)(2,1)S(1)} %collective-permute-done.12), kind=kLoop, calls=%fused_computation.14 | loop fusion | flops 10616832 | bytes 7077888 | tf_op jit(solution)/shard_map/concatenate | solution.py:17
  479.2 6.1 %gather_fusion.6 = bf16[64,128,384]{2,1,0:T(8,128)(2,1)} fusion(bf16[36,128,384]{2,1,0:T(8,128)(2,1)} %bitcast.137, s32[1024]{0:T(1024)S(1)} %pad_clamp_fusion), kind=kCustom, calls=%fused_computation.6 | custom fusion | bytes 12583168 | tf_op jit(solution)/shard_map/gather | solution.py:25
  490.7 6.3 %pad_maximum_fusion.5 = bf16[4608,384]{1,0:T(8,128)(2,1)} fusion(bf16[256,384]{1,0:T(8,128)(2,1)S(1)} %collective-permute-done.11, bf16[4096,384]{1,0:T(8,128)(2,1)S(1)} %copy-done.13, bf16[256,384]{1,0:T(8,128)(2,1)S(1)} %collective-permute-done.10), kind=kLoop, calls=%fused_computation.13 | loop fusion | flops 10616832 | bytes 7077888 | tf_op jit(solution)/shard_map/concatenate | solution.py:17
  497.0 6.1 %gather_fusion.5 = bf16[64,128,384]{2,1,0:T(8,128)(2,1)} fusion(bf16[36,128,384]{2,1,0:T(8,128)(2,1)} %bitcast.138, s32[1024]{0:T(1024)S(1)} %pad_clamp_fusion), kind=kCustom, calls=%fused_computation.5 | custom fusion | bytes 12583168 | tf_op jit(solution)/shard_map/gather | solution.py:25
  508.4 6.5 %pad_maximum_fusion.4 = bf16[4608,384]{1,0:T(8,128)(2,1)} fusion(bf16[256,384]{1,0:T(8,128)(2,1)S(1)} %collective-permute-done.9, bf16[4096,384]{1,0:T(8,128)(2,1)S(1)} %copy-done.12, bf16[256,384]{1,0:T(8,128)(2,1)S(1)} %collective-permute-done.8), kind=kLoop, calls=%fused_computation.12 | loop fusion | flops 10616832 | bytes 7077888 | tf_op jit(solution)/shard_map/concatenate | solution.py:17
  (118 shorter events, 120.3 us)
Async XLA Ops:
  7.2 71.4 %all-gather.15.cloned.1.call-start = ((), (), s32[]{:S(2)}) async-start(), calls=%async_computation.5 | async-start | bytes 3932160 | tf_op jit(solution)/shard_map/all_gather | solution.py:22
  10.9 106.1 %all-gather.13.cloned.1.call-start = ((), (), s32[]{:S(2)}) async-start(), calls=%async_computation.4 | async-start | bytes 3932160 | tf_op jit(solution)/shard_map/all_gather | solution.py:22
  11.6 146.8 %all-gather.11.cloned.1.call-start = ((), (), s32[]{:S(2)}) async-start(), calls=%async_computation.3 | async-start | bytes 3932160 | tf_op jit(solution)/shard_map/all_gather | solution.py:22
  12.4 187.9 %all-gather.9.cloned.1.call-start = ((), (), s32[]{:S(2)}) async-start(), calls=%async_computation.2 | async-start | bytes 3932160 | tf_op jit(solution)/shard_map/all_gather | solution.py:22
  23.6 52.0 %all-to-all-start.1 = ((bf16[32,2,128,128]{3,2,1,0:T(8,128)(2,1)}), bf16[32,2,128,128]{3,2,1,0:T(8,128)(2,1)S(1)}, u32[]{:S(2)}, u32[]{:S(2)}) async-start(bf16[32,2,128,128]{3,2,1,0:T(8,128)(2,1)} %param.4), calls=%async_computation.1 | async-start | bytes 4194304 | tf_op jit(solution)/shard_map/all_to_all | solution.py:35
  27.2 291.3 %all-gather.23.cloned.1.call-start = ((), (), s32[]{:S(2)}) async-start(), calls=%async_computation.9 | async-start | bytes 3932160 | tf_op jit(solution)/shard_map/all_gather | solution.py:22
  79.7 122.4 %collective-permute-start.6 = (bf16[256,384]{1,0:T(8,128)(2,1)S(1)}, bf16[256,384]{1,0:T(8,128)(2,1)S(1)}, u32[]{:S(2)}, u32[]{:S(2)}) collective-permute-start(bf16[256,384]{1,0:T(8,128)(2,1)S(1)} %get-tuple-element.28), channel_id=1, source_target_pairs={{0,4},{4,8},{8,12},{12,16},{16,20},{20,24},{24,28},{28,32},{32,36}... | collective-permute-start | bytes 589832 | tf_op jit(solution)/shard_map/ppermute | solution.py:15
  79.8 126.4 %collective-permute-start.7 = (bf16[256,384]{1,0:T(8,128)(2,1)S(1)}, bf16[256,384]{1,0:T(8,128)(2,1)S(1)}, u32[]{:S(2)}, u32[]{:S(2)}) collective-permute-start(bf16[256,384]{1,0:T(8,128)(2,1)S(1)} %get-tuple-element.29), channel_id=1, source_target_pairs={{4,0},{8,4},{12,8},{16,12},{20,16},{24,20},{28,24},{32,28},{36,32}... | collective-permute-start | bytes 589832 | tf_op jit(solution)/shard_map/ppermute | solution.py:16
  118.8 100.6 %collective-permute-start.4 = (bf16[256,384]{1,0:T(8,128)(2,1)}, bf16[256,384]{1,0:T(8,128)(2,1)S(1)}, u32[]{:S(2)}, u32[]{:S(2)}) collective-permute-start(bf16[256,384]{1,0:T(8,128)(2,1)} %get-tuple-element.26), channel_id=1, source_target_pairs={{0,4},{4,8},{8,12},{12,16},{16,20},{20,24},{24,28},{28,32},{32,36}... | collective-permute-start | bytes 589832 | tf_op jit(solution)/shard_map/ppermute | solution.py:15
  118.8 106.2 %collective-permute-start.5 = (bf16[256,384]{1,0:T(8,128)(2,1)}, bf16[256,384]{1,0:T(8,128)(2,1)S(1)}, u32[]{:S(2)}, u32[]{:S(2)}) collective-permute-start(bf16[256,384]{1,0:T(8,128)(2,1)} %get-tuple-element.27), channel_id=1, source_target_pairs={{4,0},{8,4},{12,8},{16,12},{20,16},{24,20},{28,24},{32,28},{36,32}... | collective-permute-start | bytes 589832 | tf_op jit(solution)/shard_map/ppermute | solution.py:16
  160.2 85.7 %collective-permute-start.2 = (bf16[256,384]{1,0:T(8,128)(2,1)}, bf16[256,384]{1,0:T(8,128)(2,1)S(1)}, u32[]{:S(2)}, u32[]{:S(2)}) collective-permute-start(bf16[256,384]{1,0:T(8,128)(2,1)} %get-tuple-element.24), channel_id=1, source_target_pairs={{0,4},{4,8},{8,12},{12,16},{16,20},{20,24},{24,28},{28,32},{32,36}... | collective-permute-start | bytes 589832 | tf_op jit(solution)/shard_map/ppermute | solution.py:15
  202.1 43.9 %collective-permute-start.3 = (bf16[256,384]{1,0:T(8,128)(2,1)}, bf16[256,384]{1,0:T(8,128)(2,1)S(1)}, u32[]{:S(2)}, u32[]{:S(2)}) collective-permute-start(bf16[256,384]{1,0:T(8,128)(2,1)} %get-tuple-element.25), channel_id=1, source_target_pairs={{4,0},{8,4},{12,8},{16,12},{20,16},{24,20},{28,24},{32,28},{36,32}... | collective-permute-start | bytes 589832 | tf_op jit(solution)/shard_map/ppermute | solution.py:16
  206.2 57.4 %collective-permute-start = (bf16[256,384]{1,0:T(8,128)(2,1)}, bf16[256,384]{1,0:T(8,128)(2,1)S(1)}, u32[]{:S(2)}, u32[]{:S(2)}) collective-permute-start(bf16[256,384]{1,0:T(8,128)(2,1)} %get-tuple-element.18), channel_id=1, source_target_pairs={{0,4},{4,8},{8,12},{12,16},{16,20},{20,24},{24,28},{28,32},{32,36}... | collective-permute-start | bytes 589832 | tf_op jit(solution)/shard_map/ppermute | solution.py:15
  219.4 44.2 %collective-permute-start.1 = (bf16[256,384]{1,0:T(8,128)(2,1)S(1)}, bf16[256,384]{1,0:T(8,128)(2,1)S(1)}, u32[]{:S(2)}, u32[]{:S(2)}) collective-permute-start(bf16[256,384]{1,0:T(8,128)(2,1)S(1)} %copy-done.16), channel_id=1, source_target_pairs={{4,0},{8,4},{12,8},{16,12},{20,16},{24,20},{28,24},{32,28},{36,32}... | collective-permute-start | bytes 589832 | tf_op jit(solution)/shard_map/ppermute | solution.py:16
  283.5 76.3 %all-gather.21.cloned.1.call-start = ((), (), s32[]{:S(2)}) async-start(), calls=%async_computation.8 | async-start | bytes 3932160 | tf_op jit(solution)/shard_map/all_gather | solution.py:22
  284.1 117.2 %all-gather.19.cloned.1.call-start = ((), (), s32[]{:S(2)}) async-start(), calls=%async_computation.7 | async-start | bytes 3932160 | tf_op jit(solution)/shard_map/all_gather | solution.py:22
  284.8 158.4 %all-gather.17.cloned.1.call-start = ((), (), s32[]{:S(2)}) async-start(), calls=%async_computation.6 | async-start | bytes 3932160 | tf_op jit(solution)/shard_map/all_gather | solution.py:22
  319.6 125.5 %collective-permute-start.14 = (bf16[256,384]{1,0:T(8,128)(2,1)S(1)}, bf16[256,384]{1,0:T(8,128)(2,1)S(1)}, u32[]{:S(2)}, u32[]{:S(2)}) collective-permute-start(bf16[256,384]{1,0:T(8,128)(2,1)S(1)} %get-tuple-element.12), channel_id=1, source_target_pairs={{0,4},{4,8},{8,12},{12,16},{16,20},{20,24},{24,28},{28,32},{32,36}... | collective-permute-start | bytes 589832 | tf_op jit(solution)/shard_map/ppermute | solution.py:15
  319.7 129.5 %collective-permute-start.15 = (bf16[256,384]{1,0:T(8,128)(2,1)S(1)}, bf16[256,384]{1,0:T(8,128)(2,1)S(1)}, u32[]{:S(2)}, u32[]{:S(2)}) collective-permute-start(bf16[256,384]{1,0:T(8,128)(2,1)S(1)} %get-tuple-element.13), channel_id=1, source_target_pairs={{4,0},{8,4},{12,8},{16,12},{20,16},{24,20},{28,24},{32,28},{36,32}... | collective-permute-start | bytes 589832 | tf_op jit(solution)/shard_map/ppermute | solution.py:16
  361.6 106.1 %collective-permute-start.12 = (bf16[256,384]{1,0:T(8,128)(2,1)}, bf16[256,384]{1,0:T(8,128)(2,1)S(1)}, u32[]{:S(2)}, u32[]{:S(2)}) collective-permute-start(bf16[256,384]{1,0:T(8,128)(2,1)} %get-tuple-element.10), channel_id=1, source_target_pairs={{0,4},{4,8},{8,12},{12,16},{16,20},{20,24},{24,28},{28,32},{32,36}... | collective-permute-start | bytes 589832 | tf_op jit(solution)/shard_map/ppermute | solution.py:15
  361.6 111.1 %collective-permute-start.13 = (bf16[256,384]{1,0:T(8,128)(2,1)}, bf16[256,384]{1,0:T(8,128)(2,1)S(1)}, u32[]{:S(2)}, u32[]{:S(2)}) collective-permute-start(bf16[256,384]{1,0:T(8,128)(2,1)} %get-tuple-element.11), channel_id=1, source_target_pairs={{4,0},{8,4},{12,8},{16,12},{20,16},{24,20},{28,24},{32,28},{36,32}... | collective-permute-start | bytes 589832 | tf_op jit(solution)/shard_map/ppermute | solution.py:16
  403.1 87.6 %collective-permute-start.10 = (bf16[256,384]{1,0:T(8,128)(2,1)}, bf16[256,384]{1,0:T(8,128)(2,1)S(1)}, u32[]{:S(2)}, u32[]{:S(2)}) collective-permute-start(bf16[256,384]{1,0:T(8,128)(2,1)} %get-tuple-element.8), channel_id=1, source_target_pairs={{0,4},{4,8},{8,12},{12,16},{16,20},{20,24},{24,28},{28,32},{32,36}... | collective-permute-start | bytes 589832 | tf_op jit(solution)/shard_map/ppermute | solution.py:15
  445.0 45.6 %collective-permute-start.11 = (bf16[256,384]{1,0:T(8,128)(2,1)}, bf16[256,384]{1,0:T(8,128)(2,1)S(1)}, u32[]{:S(2)}, u32[]{:S(2)}) collective-permute-start(bf16[256,384]{1,0:T(8,128)(2,1)} %get-tuple-element.9), channel_id=1, source_target_pairs={{4,0},{8,4},{12,8},{16,12},{20,16},{24,20},{28,24},{32,28},{36,32}... | collective-permute-start | bytes 589832 | tf_op jit(solution)/shard_map/ppermute | solution.py:16
  449.2 59.2 %collective-permute-start.8 = (bf16[256,384]{1,0:T(8,128)(2,1)}, bf16[256,384]{1,0:T(8,128)(2,1)S(1)}, u32[]{:S(2)}, u32[]{:S(2)}) collective-permute-start(bf16[256,384]{1,0:T(8,128)(2,1)} %get-tuple-element.6), channel_id=1, source_target_pairs={{0,4},{4,8},{8,12},{12,16},{16,20},{20,24},{24,28},{28,32},{32,36}... | collective-permute-start | bytes 589832 | tf_op jit(solution)/shard_map/ppermute | solution.py:15
  (20 other events, 131.7 us)
Sparse Core Ops, SparseCore 0:
  11.0 64.1 all-gather.14
  76.8 40.1 all-gather.12
  118.6 39.7 all-gather.10
  160.5 39.7 all-gather.8
  283.6 34.8 all-gather.22
  320.0 39.7 all-gather.20
  361.5 39.7 all-gather.18
  403.5 39.7 all-gather.16
where the time goes:
time: 542 us; the launch traced here: 536 us
  waiting for transfers between devices  298 us (55%)
  local copies, waits for them, and re-layouts  70.3 us (13%)
  other arithmetic  61 us (11%)
  starting transfers between devices  43.2 us (8%)
  matrix products  37.6 us (7%)
  between operations  14.8 us (3%)
  blocking collectives  10.5 us (2%)
    all_gather x8, waiting for transfers between devices, own_rows(): panel = lax.all_gather(chunk, 'layer', axis=0, tiled=True)  246 us
    concatenate x8, other arithmetic, padded(): return jnp.concatenate([before, array, after], axis=0)  53.2 us
    gather x8, local copies, waits for them, and re-layouts, own_rows(): picked = blocks[rel_own]  48.5 us
    all_to_all x1, waiting for transfers between devices, shards(): h_own = lax.all_to_all(h_blocks, 'layer', 0, 1, tiled=True)  48.1 us
    ppermute x8, starting transfers between devices, padded(): after = lax.ppermute(array[:width], 'grid', down)  39.1 us
    dot_general x8, matrix products, own_rows(): jnp.einsum('rsij,rsjc->ric', h_own, picked, preferred_element_type=jnp.fl...  37.6 us
    slice x8, local copies, waits for them, and re-layouts, padded(): before = lax.ppermute(array[length - width:], 'grid', up)  13 us
  transfers between devices with their start and end apart: 25, of which 8 were waited for; matrix products, arithmetic and copies ran while one was open for 23% of the time, Pallas kernels for 0%

commit v1 on v0

--- a/solution.py
+++ b/solution.py
@@ -19,7 +19,15 @@
 
 def own_rows(h_own, rel_own, chunk):
     block_size = h_own.shape[2]
-    panel = lax.all_gather(chunk, "layer", axis=0, tiled=True)
+
+    def strips_all_draft(original, mesh_ax):
+        out_arr = tuple((original for _ in range(lax.axis_size(mesh_ax))))
+        return jnp.concatenate(
+            lax.all_to_all(jnp.stack(out_arr), axis_name=mesh_ax, split_axis=0, concat_axis=0),
+            axis=0,
+        )
+
+    panel = strips_all_draft(chunk, "layer")
     wide = padded(panel, HB * block_size)
     blocks = wide.reshape(wide.shape[0] // block_size, block_size, chunk.shape[1])
     picked = blocks[rel_own]

time: 542 us -> 522 us (0.963)
  waiting for transfers between devices: 298 us -> 50.1 us
  blocking collectives: 10.5 us -> 235 us
  between operations: 14.8 us -> 1.08 us
  starting transfers between devices: 43.2 us -> 53 us
  local copies, waits for them, and re-layouts: 70.3 us -> 76 us
    all_gather x8 -> x0, waiting for transfers between devices: 246 us -> none  [own_rows(): panel = lax.all_gather(chunk, 'layer', axis=0, tiled=True)]
    all_to_all x0 -> x6, blocking collectives: none -> 224 us  [strips_all_draft(): lax.all_to_all(jnp.stack(out_arr), axis_name=mesh_ax, split_axis=0, conca...]
    all_to_all x0 -> x2, waiting for transfers between devices: none -> 28.2 us  [strips_all_draft(): lax.all_to_all(jnp.stack(out_arr), axis_name=mesh_ax, split_axis=0, conca...]
    all_to_all x1, waiting for transfers between devices: 48.1 us -> 21.8 us  [shards(): h_own = lax.all_to_all(h_blocks, 'layer', 0, 1, tiled=True)]
    all_to_all x0 -> x2, starting transfers between devices: none -> 9.32 us  [strips_all_draft(): lax.all_to_all(jnp.stack(out_arr), axis_name=mesh_ax, split_axis=0, conca...]
    another operation x0 -> x8, local copies, waits for them, and re-layouts: none -> 7.17 us  [strips_all_draft(): jnp.stack(out_arr)]
  transfers between devices with their start and end apart: 25 -> 19, of which waited for: 8 -> 3; matrix products, arithmetic and copies ran while one was open for 23% -> 25% of each run, Pallas kernels for 0% -> 0%
where the time goes in v1:
time: 522 us; the launch traced here: 514 us
  blocking collectives  235 us (45%)
  local copies, waits for them, and re-layouts  76 us (15%)
  other arithmetic  62.2 us (12%)
  starting transfers between devices  53 us (10%)
  waiting for transfers between devices  50.1 us (10%)
  matrix products  37.5 us (7%)
    all_to_all x6, blocking collectives, strips_all_draft(): lax.all_to_all(jnp.stack(out_arr), axis_name=mesh_ax, split_axis=0, conca...  224 us
    concatenate x8, other arithmetic, padded(): return jnp.concatenate([before, array, after], axis=0)  55.1 us
    gather x8, local copies, waits for them, and re-layouts, own_rows(): picked = blocks[rel_own]  48.6 us
    dot_general x8, matrix products, own_rows(): jnp.einsum('rsij,rsjc->ric', h_own, picked, preferred_element_type=jnp.fl...  37.5 us
    ppermute x8, starting transfers between devices, padded(): after = lax.ppermute(array[:width], 'grid', down)  36.9 us
    all_to_all x2, waiting for transfers between devices, strips_all_draft(): lax.all_to_all(jnp.stack(out_arr), axis_name=mesh_ax, split_axis=0, conca...  28.2 us
    all_to_all x1, waiting for transfers between devices, shards(): h_own = lax.all_to_all(h_blocks, 'layer', 0, 1, tiled=True)  21.8 us
    slice x8, local copies, waits for them, and re-layouts, padded(): before = lax.ppermute(array[length - width:], 'grid', up)  13 us
  transfers between devices with their start and end apart: 19, of which 3 were waited for; matrix products, arithmetic and copies ran while one was open for 25% of the time, Pallas kernels for 0%

profile of v1, /device:TPU:0, one launch (start us, length us, event | category | flops | bytes accessed | tf_op | source)
XLA Modules:
  0.0 514.4 jit_solution(13680437825567032629)
XLA Ops:
  1.4 10.5 %all_to_all.77 = s32[4,8,2]{1,2,0:T(2,128)S(1)} all-to-all(s32[4,8,2]{1,2,0:T(2,128)S(1)} %copy.9), channel_id=1, replica_groups=mesh['grid'=32,'layer'=4] {'layer'}, dimensions={0} | all-to-all | bytes 512 | tf_op jit(solution)/shard_map/all_to_all | solution.py:44
  18.9 21.8 %all-to-all-done.2 = bf16[32,2,128,128]{3,2,1,0:T(8,128)(2,1)S(1)} async-done(((bf16[32,2,128,128]{3,2,1,0:T(8,128)(2,1)}), bf16[32,2,128,128]{3,2,1,0:T(8,128)(2,1)S(1)}, u32[]{:S(2)}, u32[]{:S(2)}) %all-to-all-start.2) | async-done | bytes 2097184 | tf_op jit(solution)/shard_map/all_to_all | solution.py:43
  42.6 39.0 %all_to_all.78 = bf16[4,1024,384]{2,1,0:T(8,128)(2,1)} all-to-all(bf16[4,1024,384]{2,1,0:T(8,128)(2,1)S(1)} %stack.19), channel_id=1, replica_groups=mesh['grid'=32,'layer'=4] {'layer'}, dimensions={0} | all-to-all | bytes 6291456 | tf_op jit(solution)/shard_map/all_to_all | solution.py:26
  82.0 38.0 %all_to_all.79 = bf16[4,1024,384]{2,1,0:T(8,128)(2,1)} all-to-all(bf16[4,1024,384]{2,1,0:T(8,128)(2,1)S(1)} %stack.18), channel_id=1, replica_groups=mesh['grid'=32,'layer'=4] {'layer'}, dimensions={0} | all-to-all | bytes 6291456 | tf_op jit(solution)/shard_map/all_to_all | solution.py:26
  120.3 37.0 %all_to_all.80 = bf16[4,1024,384]{2,1,0:T(8,128)(2,1)} all-to-all(bf16[4,1024,384]{2,1,0:T(8,128)(2,1)S(1)} %stack.17), channel_id=1, replica_groups=mesh['grid'=32,'layer'=4] {'layer'}, dimensions={0} | all-to-all | bytes 6291456 | tf_op jit(solution)/shard_map/all_to_all | solution.py:26
  180.8 15.7 %all-to-all-done = bf16[4,1024,384]{2,1,0:T(8,128)(2,1)} async-done(((bf16[4,1024,384]{2,1,0:T(8,128)(2,1)}), bf16[4,1024,384]{2,1,0:T(8,128)(2,1)}, u32[]{:S(2)}, u32[]{:S(2)}) %all-to-all-start) | async-done | bytes 3145760 | tf_op jit(solution)/shard_map/all_to_all | solution.py:26
  198.8 7.1 %pad_maximum_fusion.3 = bf16[4608,384]{1,0:T(8,128)(2,1)} fusion(bf16[256,384]{1,0:T(8,128)(2,1)S(1)} %collective-permute-done.7, bf16[4096,384]{1,0:T(8,128)(2,1)} %bitcast.156, bf16[256,384]{1,0:T(8,128)(2,1)S(1)} %collective-permute-done.6), kind=kLoop, calls=%fused_computation.11 | loop fusion | flops 10616832 | bytes 7077888 | tf_op jit(solution)/shard_map/concatenate | solution.py:17
  216.9 7.1 %pad_maximum_fusion.2 = bf16[4608,384]{1,0:T(8,128)(2,1)} fusion(bf16[256,384]{1,0:T(8,128)(2,1)S(1)} %collective-permute-done.5, bf16[4096,384]{1,0:T(8,128)(2,1)} %bitcast.152, bf16[256,384]{1,0:T(8,128)(2,1)S(1)} %collective-permute-done.4), kind=kLoop, calls=%fused_computation.10 | loop fusion | flops 10616832 | bytes 7077888 | tf_op jit(solution)/shard_map/concatenate | solution.py:17
  224.0 6.2 %gather_fusion.2 = bf16[64,128,384]{2,1,0:T(8,128)(2,1)} fusion(bf16[36,128,384]{2,1,0:T(8,128)(2,1)} %bitcast.141, s32[1024]{0:T(1024)S(1)} %pad_clamp_fusion), kind=kCustom, calls=%fused_computation.2 | custom fusion | bytes 12583168 | tf_op jit(solution)/shard_map/gather | solution.py:33
  238.1 6.3 %pad_maximum_fusion.1 = bf16[4608,384]{1,0:T(8,128)(2,1)} fusion(bf16[256,384]{1,0:T(8,128)(2,1)S(1)} %collective-permute-done.3, bf16[4096,384]{1,0:T(8,128)(2,1)S(1)} %bitcast.148, bf16[256,384]{1,0:T(8,128)(2,1)S(1)} %collective-permute-done.2), kind=kLoop, calls=%fused_computation.9 | loop fusion | flops 10616832 | bytes 7077888 | tf_op jit(solution)/shard_map/concatenate | solution.py:17
  244.3 6.1 %gather_fusion.1 = bf16[64,128,384]{2,1,0:T(8,128)(2,1)} fusion(bf16[36,128,384]{2,1,0:T(8,128)(2,1)} %bitcast.142, s32[1024]{0:T(1024)S(1)} %pad_clamp_fusion), kind=kCustom, calls=%fused_computation.1 | custom fusion | bytes 12583168 | tf_op jit(solution)/shard_map/gather | solution.py:33
  255.7 7.3 %pad_maximum_fusion = bf16[4608,384]{1,0:T(8,128)(2,1)} fusion(bf16[256,384]{1,0:T(8,128)(2,1)S(1)} %collective-permute-done.1, bf16[4096,384]{1,0:T(8,128)(2,1)} %bitcast, bf16[256,384]{1,0:T(8,128)(2,1)S(1)} %collective-permute-done), kind=kLoop, calls=%fused_computation.8 | loop fusion | flops 10616832 | bytes 7077888 | tf_op jit(solution)/shard_map/concatenate | solution.py:17
  262.9 6.1 %gather_fusion = bf16[64,128,384]{2,1,0:T(8,128)(2,1)} fusion(bf16[36,128,384]{2,1,0:T(8,128)(2,1)} %bitcast.143, s32[1024]{0:T(1024)S(1)} %pad_clamp_fusion), kind=kCustom, calls=%fused_computation | custom fusion | bytes 12583168 | tf_op jit(solution)/shard_map/gather | solution.py:33
  275.2 37.7 %all_to_all.81 = bf16[4,1024,384]{2,1,0:T(8,128)(2,1)} all-to-all(bf16[4,1024,384]{2,1,0:T(8,128)(2,1)S(1)} %stack.23), channel_id=1, replica_groups=mesh['grid'=32,'layer'=4] {'layer'}, dimensions={0} | all-to-all | bytes 6291456 | tf_op jit(solution)/shard_map/all_to_all | solution.py:26
  313.3 36.6 %all_to_all.82 = bf16[4,1024,384]{2,1,0:T(8,128)(2,1)} all-to-all(bf16[4,1024,384]{2,1,0:T(8,128)(2,1)S(1)} %stack.22), channel_id=1, replica_groups=mesh['grid'=32,'layer'=4] {'layer'}, dimensions={0} | all-to-all | bytes 6291456 | tf_op jit(solution)/shard_map/all_to_all | solution.py:26
  350.2 35.7 %all_to_all.83 = bf16[4,1024,384]{2,1,0:T(8,128)(2,1)} all-to-all(bf16[4,1024,384]{2,1,0:T(8,128)(2,1)S(1)} %stack.21), channel_id=1, replica_groups=mesh['grid'=32,'layer'=4] {'layer'}, dimensions={0} | all-to-all | bytes 6291456 | tf_op jit(solution)/shard_map/all_to_all | solution.py:26
  396.7 6.1 %collective-permute-start.15 = (bf16[256,384]{1,0:T(8,128)(2,1)S(1)}, bf16[256,384]{1,0:T(8,128)(2,1)S(1)}, u32[]{:S(2)}, u32[]{:S(2)}) collective-permute-start(bf16[256,384]{1,0:T(8,128)(2,1)S(1)} %get-tuple-element.13), channel_id=1, source_target_pairs={{4,0},{8,4},{12,8},{16,12},{20,16},{24,20},{28,24},{32,28},{36,32}... | collective-permute-start | bytes 589832 | tf_op jit(solution)/shard_map/ppermute | solution.py:16
  411.5 12.6 %all-to-all-done.6 = bf16[4,1024,384]{2,1,0:T(8,128)(2,1)} async-done(((bf16[4,1024,384]{2,1,0:T(8,128)(2,1)}), bf16[4,1024,384]{2,1,0:T(8,128)(2,1)}, u32[]{:S(2)}, u32[]{:S(2)}) %all-to-all-start.6) | async-done | bytes 3145760 | tf_op jit(solution)/shard_map/all_to_all | solution.py:26
  425.9 8.0 %collective-permute-start.11 = (bf16[256,384]{1,0:T(8,128)(2,1)}, bf16[256,384]{1,0:T(8,128)(2,1)S(1)}, u32[]{:S(2)}, u32[]{:S(2)}) collective-permute-start(bf16[256,384]{1,0:T(8,128)(2,1)} %get-tuple-element.9), channel_id=1, source_target_pairs={{4,0},{8,4},{12,8},{16,12},{20,16},{24,20},{28,24},{32,28},{36,32}... | collective-permute-start | bytes 589832 | tf_op jit(solution)/shard_map/ppermute | solution.py:16
  433.9 7.5 %pad_maximum_fusion.7 = bf16[4608,384]{1,0:T(8,128)(2,1)} fusion(bf16[256,384]{1,0:T(8,128)(2,1)S(1)} %collective-permute-done.15, bf16[4096,384]{1,0:T(8,128)(2,1)} %bitcast.158, bf16[256,384]{1,0:T(8,128)(2,1)S(1)} %collective-permute-done.14), kind=kLoop, calls=%fused_computation.15 | loop fusion | flops 10616832 | bytes 7077888 | tf_op jit(solution)/shard_map/concatenate | solution.py:17
  458.0 6.2 %pad_maximum_fusion.6 = bf16[4608,384]{1,0:T(8,128)(2,1)} fusion(bf16[256,384]{1,0:T(8,128)(2,1)S(1)} %collective-permute-done.13, bf16[4096,384]{1,0:T(8,128)(2,1)S(1)} %bitcast.154, bf16[256,384]{1,0:T(8,128)(2,1)S(1)} %collective-permute-done.12), kind=kLoop, calls=%fused_computation.14 | loop fusion | flops 10616832 | bytes 7077888 | tf_op jit(solution)/shard_map/concatenate | solution.py:17
  475.7 6.3 %pad_maximum_fusion.5 = bf16[4608,384]{1,0:T(8,128)(2,1)} fusion(bf16[256,384]{1,0:T(8,128)(2,1)S(1)} %collective-permute-done.11, bf16[4096,384]{1,0:T(8,128)(2,1)S(1)} %bitcast.150, bf16[256,384]{1,0:T(8,128)(2,1)S(1)} %collective-permute-done.10), kind=kLoop, calls=%fused_computation.13 | loop fusion | flops 10616832 | bytes 7077888 | tf_op jit(solution)/shard_map/concatenate | solution.py:17
  493.1 7.3 %pad_maximum_fusion.4 = bf16[4608,384]{1,0:T(8,128)(2,1)} fusion(bf16[256,384]{1,0:T(8,128)(2,1)S(1)} %collective-permute-done.9, bf16[4096,384]{1,0:T(8,128)(2,1)} %bitcast.35, bf16[256,384]{1,0:T(8,128)(2,1)S(1)} %collective-permute-done.8), kind=kLoop, calls=%fused_computation.12 | loop fusion | flops 10616832 | bytes 7077888 | tf_op jit(solution)/shard_map/concatenate | solution.py:17
  500.5 6.1 %gather_fusion.4 = bf16[64,128,384]{2,1,0:T(8,128)(2,1)} fusion(bf16[36,128,384]{2,1,0:T(8,128)(2,1)} %bitcast.139, s32[1024]{0:T(1024)S(1)} %pad_clamp_fusion), kind=kCustom, calls=%fused_computation.4 | custom fusion | bytes 12583168 | tf_op jit(solution)/shard_map/gather | solution.py:33
  (114 shorter events, 134.8 us)
Async XLA Ops:
  11.9 28.8 %all-to-all-start.2 = ((bf16[32,2,128,128]{3,2,1,0:T(8,128)(2,1)}), bf16[32,2,128,128]{3,2,1,0:T(8,128)(2,1)S(1)}, u32[]{:S(2)}, u32[]{:S(2)}) async-start(bf16[32,2,128,128]{3,2,1,0:T(8,128)(2,1)} %param.4), calls=%async_computation.2 | async-start | bytes 4194304 | tf_op jit(solution)/shard_map/all_to_all | solution.py:43
  40.7 41.0 %copy-start.5 = (bf16[32,2,128,128]{3,2,1,0:T(8,128)(2,1)}, bf16[32,2,128,128]{3,2,1,0:T(8,128)(2,1)S(1)}, u32[]{:S(2)}) copy-start(bf16[32,2,128,128]{3,2,1,0:T(8,128)(2,1)S(1)} %all-to-all-done.2) | copy-start | bytes 6291460
  42.6 39.0 %copy-start.17 = (bf16[1024,384]{1,0:T(8,128)(2,1)S(1)}, bf16[1024,384]{1,0:T(8,128)(2,1)}, u32[]{:S(2)}) copy-start(bf16[1024,384]{1,0:T(8,128)(2,1)} %get-tuple-element.23) | copy-start | bytes 2359300
  159.2 37.2 %all-to-all-start = ((bf16[4,1024,384]{2,1,0:T(8,128)(2,1)}), bf16[4,1024,384]{2,1,0:T(8,128)(2,1)}, u32[]{:S(2)}, u32[]{:S(2)}) async-start(bf16[4,1024,384]{2,1,0:T(8,128)(2,1)} %stack.16), calls=%async_computation | async-start | bytes 6291456 | tf_op jit(solution)/shard_map/all_to_all | solution.py:26
  167.0 31.3 %collective-permute-start.6 = (bf16[256,384]{1,0:T(8,128)(2,1)S(1)}, bf16[256,384]{1,0:T(8,128)(2,1)S(1)}, u32[]{:S(2)}, u32[]{:S(2)}) collective-permute-start(bf16[256,384]{1,0:T(8,128)(2,1)S(1)} %get-tuple-element.28), channel_id=1, source_target_pairs={{0,4},{4,8},{8,12},{12,16},{16,20},{20,24},{24,28},{28,32},{32,36}... | collective-permute-start | bytes 589832 | tf_op jit(solution)/shard_map/ppermute | solution.py:15
  167.0 31.2 %collective-permute-start.7 = (bf16[256,384]{1,0:T(8,128)(2,1)S(1)}, bf16[256,384]{1,0:T(8,128)(2,1)S(1)}, u32[]{:S(2)}, u32[]{:S(2)}) collective-permute-start(bf16[256,384]{1,0:T(8,128)(2,1)S(1)} %get-tuple-element.29), channel_id=1, source_target_pairs={{4,0},{8,4},{12,8},{16,12},{20,16},{24,20},{28,24},{32,28},{36,32}... | collective-permute-start | bytes 589832 | tf_op jit(solution)/shard_map/ppermute | solution.py:16
  173.9 38.0 %collective-permute-start.4 = (bf16[256,384]{1,0:T(8,128)(2,1)}, bf16[256,384]{1,0:T(8,128)(2,1)S(1)}, u32[]{:S(2)}, u32[]{:S(2)}) collective-permute-start(bf16[256,384]{1,0:T(8,128)(2,1)} %get-tuple-element.26), channel_id=1, source_target_pairs={{0,4},{4,8},{8,12},{12,16},{16,20},{20,24},{24,28},{28,32},{32,36}... | collective-permute-start | bytes 589832 | tf_op jit(solution)/shard_map/ppermute | solution.py:15
  173.9 43.0 %collective-permute-start.5 = (bf16[256,384]{1,0:T(8,128)(2,1)}, bf16[256,384]{1,0:T(8,128)(2,1)S(1)}, u32[]{:S(2)}, u32[]{:S(2)}) collective-permute-start(bf16[256,384]{1,0:T(8,128)(2,1)} %get-tuple-element.27), channel_id=1, source_target_pairs={{4,0},{8,4},{12,8},{16,12},{20,16},{24,20},{28,24},{32,28},{36,32}... | collective-permute-start | bytes 589832 | tf_op jit(solution)/shard_map/ppermute | solution.py:16
  180.8 57.3 %collective-permute-start.2 = (bf16[256,384]{1,0:T(8,128)(2,1)}, bf16[256,384]{1,0:T(8,128)(2,1)S(1)}, u32[]{:S(2)}, u32[]{:S(2)}) collective-permute-start(bf16[256,384]{1,0:T(8,128)(2,1)} %get-tuple-element.24), channel_id=1, source_target_pairs={{0,4},{4,8},{8,12},{12,16},{16,20},{20,24},{24,28},{28,32},{32,36}... | collective-permute-start | bytes 589832 | tf_op jit(solution)/shard_map/ppermute | solution.py:15
  198.3 39.8 %collective-permute-start.3 = (bf16[256,384]{1,0:T(8,128)(2,1)}, bf16[256,384]{1,0:T(8,128)(2,1)S(1)}, u32[]{:S(2)}, u32[]{:S(2)}) collective-permute-start(bf16[256,384]{1,0:T(8,128)(2,1)} %get-tuple-element.25), channel_id=1, source_target_pairs={{4,0},{8,4},{12,8},{16,12},{20,16},{24,20},{28,24},{32,28},{36,32}... | collective-permute-start | bytes 589832 | tf_op jit(solution)/shard_map/ppermute | solution.py:16
  198.3 57.4 %collective-permute-start = (bf16[256,384]{1,0:T(8,128)(2,1)}, bf16[256,384]{1,0:T(8,128)(2,1)S(1)}, u32[]{:S(2)}, u32[]{:S(2)}) collective-permute-start(bf16[256,384]{1,0:T(8,128)(2,1)} %get-tuple-element.18), channel_id=1, source_target_pairs={{0,4},{4,8},{8,12},{12,16},{16,20},{20,24},{24,28},{28,32},{32,36}... | collective-permute-start | bytes 589832 | tf_op jit(solution)/shard_map/ppermute | solution.py:15
  211.9 43.7 %collective-permute-start.1 = (bf16[256,384]{1,0:T(8,128)(2,1)S(1)}, bf16[256,384]{1,0:T(8,128)(2,1)S(1)}, u32[]{:S(2)}, u32[]{:S(2)}) collective-permute-start(bf16[256,384]{1,0:T(8,128)(2,1)S(1)} %copy-done.18), channel_id=1, source_target_pairs={{4,0},{8,4},{12,8},{16,12},{20,16},{24,20},{28,24},{32,28},{36,32}... | collective-permute-start | bytes 589832 | tf_op jit(solution)/shard_map/ppermute | solution.py:16
  274.9 38.1 %copy-start.13 = (bf16[1024,384]{1,0:T(8,128)(2,1)}, bf16[1024,384]{1,0:T(8,128)(2,1)S(1)}, u32[]{:S(2)}) copy-start(bf16[1024,384]{1,0:T(8,128)(2,1)S(1)} %get-tuple-element.16) | copy-start | bytes 2359300
  274.9 38.1 %copy-start.14 = (bf16[1024,384]{1,0:T(8,128)(2,1)}, bf16[1024,384]{1,0:T(8,128)(2,1)S(1)}, u32[]{:S(2)}) copy-start(bf16[1024,384]{1,0:T(8,128)(2,1)S(1)} %get-tuple-element.17) | copy-start | bytes 2359300
  274.9 75.0 %copy-start.12 = (bf16[1024,384]{1,0:T(8,128)(2,1)}, bf16[1024,384]{1,0:T(8,128)(2,1)S(1)}, u32[]{:S(2)}) copy-start(bf16[1024,384]{1,0:T(8,128)(2,1)S(1)} %get-tuple-element.15) | copy-start | bytes 2359300
  387.8 36.3 %all-to-all-start.6 = ((bf16[4,1024,384]{2,1,0:T(8,128)(2,1)}), bf16[4,1024,384]{2,1,0:T(8,128)(2,1)}, u32[]{:S(2)}, u32[]{:S(2)}) async-start(bf16[4,1024,384]{2,1,0:T(8,128)(2,1)} %stack.20), calls=%async_computation.6 | async-start | bytes 6291456 | tf_op jit(solution)/shard_map/all_to_all | solution.py:26
  396.6 29.3 %collective-permute-start.14 = (bf16[256,384]{1,0:T(8,128)(2,1)S(1)}, bf16[256,384]{1,0:T(8,128)(2,1)S(1)}, u32[]{:S(2)}, u32[]{:S(2)}) collective-permute-start(bf16[256,384]{1,0:T(8,128)(2,1)S(1)} %get-tuple-element.12), channel_id=1, source_target_pairs={{0,4},{4,8},{8,12},{12,16},{16,20},{20,24},{24,28},{28,32},{32,36}... | collective-permute-start | bytes 589832 | tf_op jit(solution)/shard_map/ppermute | solution.py:15
  396.7 37.3 %collective-permute-start.15 = (bf16[256,384]{1,0:T(8,128)(2,1)S(1)}, bf16[256,384]{1,0:T(8,128)(2,1)S(1)}, u32[]{:S(2)}, u32[]{:S(2)}) collective-permute-start(bf16[256,384]{1,0:T(8,128)(2,1)S(1)} %get-tuple-element.13), channel_id=1, source_target_pairs={{4,0},{8,4},{12,8},{16,12},{20,16},{24,20},{28,24},{32,28},{36,32}... | collective-permute-start | bytes 589832 | tf_op jit(solution)/shard_map/ppermute | solution.py:16
  404.7 48.3 %collective-permute-start.12 = (bf16[256,384]{1,0:T(8,128)(2,1)}, bf16[256,384]{1,0:T(8,128)(2,1)S(1)}, u32[]{:S(2)}, u32[]{:S(2)}) collective-permute-start(bf16[256,384]{1,0:T(8,128)(2,1)} %get-tuple-element.10), channel_id=1, source_target_pairs={{0,4},{4,8},{8,12},{12,16},{16,20},{20,24},{24,28},{28,32},{32,36}... | collective-permute-start | bytes 589832 | tf_op jit(solution)/shard_map/ppermute | solution.py:15
  407.2 50.8 %collective-permute-start.13 = (bf16[256,384]{1,0:T(8,128)(2,1)}, bf16[256,384]{1,0:T(8,128)(2,1)S(1)}, u32[]{:S(2)}, u32[]{:S(2)}) collective-permute-start(bf16[256,384]{1,0:T(8,128)(2,1)} %get-tuple-element.11), channel_id=1, source_target_pairs={{4,0},{8,4},{12,8},{16,12},{20,16},{24,20},{28,24},{32,28},{36,32}... | collective-permute-start | bytes 589832 | tf_op jit(solution)/shard_map/ppermute | solution.py:16
  411.5 64.1 %collective-permute-start.10 = (bf16[256,384]{1,0:T(8,128)(2,1)}, bf16[256,384]{1,0:T(8,128)(2,1)S(1)}, u32[]{:S(2)}, u32[]{:S(2)}) collective-permute-start(bf16[256,384]{1,0:T(8,128)(2,1)} %get-tuple-element.8), channel_id=1, source_target_pairs={{0,4},{4,8},{8,12},{12,16},{16,20},{20,24},{24,28},{28,32},{32,36}... | collective-permute-start | bytes 589832 | tf_op jit(solution)/shard_map/ppermute | solution.py:15
  425.9 49.8 %collective-permute-start.11 = (bf16[256,384]{1,0:T(8,128)(2,1)}, bf16[256,384]{1,0:T(8,128)(2,1)S(1)}, u32[]{:S(2)}, u32[]{:S(2)}) collective-permute-start(bf16[256,384]{1,0:T(8,128)(2,1)} %get-tuple-element.9), channel_id=1, source_target_pairs={{4,0},{8,4},{12,8},{16,12},{20,16},{24,20},{28,24},{32,28},{36,32}... | collective-permute-start | bytes 589832 | tf_op jit(solution)/shard_map/ppermute | solution.py:16
  433.9 59.2 %collective-permute-start.8 = (bf16[256,384]{1,0:T(8,128)(2,1)}, bf16[256,384]{1,0:T(8,128)(2,1)S(1)}, u32[]{:S(2)}, u32[]{:S(2)}) collective-permute-start(bf16[256,384]{1,0:T(8,128)(2,1)} %get-tuple-element.6), channel_id=1, source_target_pairs={{0,4},{4,8},{8,12},{12,16},{16,20},{20,24},{24,28},{28,32},{32,36}... | collective-permute-start | bytes 589832 | tf_op jit(solution)/shard_map/ppermute | solution.py:15
  452.9 40.2 %collective-permute-start.9 = (bf16[256,384]{1,0:T(8,128)(2,1)S(1)}, bf16[256,384]{1,0:T(8,128)(2,1)S(1)}, u32[]{:S(2)}, u32[]{:S(2)}) collective-permute-start(bf16[256,384]{1,0:T(8,128)(2,1)S(1)} %copy-done.19), channel_id=1, source_target_pairs={{4,0},{8,4},{12,8},{16,12},{20,16},{24,20},{28,24},{32,28},{36,32}... | collective-permute-start | bytes 589832 | tf_op jit(solution)/shard_map/ppermute | solution.py:16
  (15 other events, 109.2 us)
